TPU v7x, 256 devices: a whole 4x4x8 slice. The times are simulated.
256 devices in a mesh: dp: 16 (over z_lo, y), tensor: 16 (over x, z_hi, core).
Axes of the slice: x: 4, y: 4, z: 8 (z_hi: 2, z_lo: 4; z = z_hi * 4 + z_lo), core: 2. Of those that a mesh axis runs over, the one named last changes fastest.
Arguments:
- hidden: bfloat16 [12288, 2048], P(('dp', 'tensor')), may hold values from -6 to 6
- lengths: int32 [64], replicated, may hold values from 1 to 384, as said below
- prefix_id: int32 [64], replicated, may hold values from 0 to 1
- placement_perm: int32 [64], replicated, may hold values from 0 to 63, as said below
- prefix_owner: int32 [2], replicated, may hold values from 0 to 15, as said below
- prefix_cache: bfloat16 [16, 2, 4096, 2048], P('dp', None, None, 'tensor'), may hold values from -400 to 400
- qkv_weight: bfloat16 [3, 2048, 2048], P(None, None, 'tensor')
- q_gain: float32 [2048], replicated, may hold values from 0.1 to 1.9
- k_gain: float32 [2048], replicated, may hold values from 0.1 to 1.9
- out_weight: bfloat16 [2048, 2048], P('tensor'), may hold values from -0.125 to 0.125
- attn_gain: float32 [2048], replicated, may hold values from 0.1 to 1.9
- gate_up_weight: bfloat16 [2, 2048, 8192], P(None, None, 'tensor'), may hold values from -0.125 to 0.125
- down_weight: bfloat16 [8192, 2048], P('tensor'), may hold values from -0.0625 to 0.0625
- mlp_gain: float32 [2048], replicated, may hold values from 0.1 to 1.9
Outputs:
- hidden_out: bfloat16 [12288, 2048], P(('dp', 'tensor'))
- suffix_kv: bfloat16 [2, 12288, 2048], P(None, 'dp', 'tensor')
Inputs may be any that keep to these rules, and one draw needn't show every extreme that they name: `lengths`: the requests that placement_perm puts into one group hold at most 768 tokens together; in every draw some group holds exactly 768. `placement_perm`: A permutation of the 64 requests. `prefix_owner`: two different dp indices, one of which is always the last dp index.
All inputs are finite; a program needn't handle non-finite values.
Results may differ from a plain program's by a relative error of at most 0.025.
Values may be sent and summed in bfloat16 or wider, within the bound.
No kernel may reach another device: no remote copies, remote signals or barrier semaphores. Data moves between devices by JAX's collectives and lax.ppermute only.
A program may use at most 128 MiB of HBM per device.

v0:
```python
import jax
import jax.numpy as jnp
from jax import lax
from jax.sharding import PartitionSpec as P

D = 2048
HD = 128
CAP = 768
REQ_GRP = 4
PLEN = 4096
ROPE_BASE = 500000.0
EPSILON = 1e-06
MASKED_SCORE = -1e30


def from_root(shard, axis, root):
    mine = lax.axis_index(axis) == root
    return lax.psum(jnp.where(mine, shard, jnp.zeros_like(shard)), axis)


def slot_plan(lengths, prefix_id, placement_perm, group_index):
    requests = lax.dynamic_slice(placement_perm, (group_index * REQ_GRP,), (REQ_GRP,))
    req_sizes = jnp.take(lengths, requests)
    starts = jnp.cumsum(req_sizes) - req_sizes
    slot_ids = jnp.arange(CAP, dtype=jnp.int32)
    inside = (
        (slot_ids[None, :] >= starts[:, None]) & (slot_ids[None, :] < (starts + req_sizes)[:, None])
    ).astype(jnp.int32)
    live_slots = jnp.sum(inside, axis=0) > 0
    numbers = jnp.arange(1, REQ_GRP + 1, dtype=jnp.int32)
    owner_req = jnp.sum(inside * numbers[:, None], axis=0) - 1
    offsets = slot_ids - jnp.sum(inside * starts[:, None], axis=0)
    prefix_pick = jnp.sum(inside * jnp.take(prefix_id, requests)[:, None], axis=0)
    return (slot_ids, live_slots, owner_req, offsets, prefix_pick)


def rotate(values, offsets):
    half_dim = HD // 2
    inverse = jnp.power(ROPE_BASE, -2.0 * jnp.arange(half_dim, dtype=jnp.float32) / HD)
    angles = (offsets.astype(jnp.float32) + PLEN)[:, None] * inverse[None, :]
    cosine = jnp.cos(angles)[:, None, :]
    sine_part = jnp.sin(angles)[:, None, :]
    front_half = values[..., :half_dim]
    back_half = values[..., half_dim:]
    return jnp.concatenate(
        [front_half * cosine - back_half * sine_part, back_half * cosine + front_half * sine_part],
        axis=-1,
    )


def rms_scale(values, gain):
    mean_square = jnp.mean(values * values, axis=-1, keepdims=True)
    return values * lax.rsqrt(mean_square + EPSILON) * gain


def partial_softmax(scores, value_heads):
    running_max = jnp.max(scores, axis=-1, keepdims=True)
    weights = jnp.exp(scores - running_max)
    weight_sum = jnp.sum(weights, axis=-1, keepdims=True)
    accumulated = jnp.einsum(
        "hck,khd->hcd",
        weights.astype(jnp.bfloat16),
        value_heads,
        preferred_element_type=jnp.float32,
    )
    return (running_max, weight_sum, accumulated)


def merge_partials(partials):
    running_max = partials[0][0]
    for member in partials[1:]:
        running_max = jnp.maximum(running_max, member[0])
    weight_sum = jnp.zeros_like(partials[0][1])
    accumulated = jnp.zeros_like(partials[0][2])
    for member in partials:
        factor = jnp.exp(member[0] - running_max)
        weight_sum = weight_sum + factor * member[1]
        accumulated = accumulated + factor * member[2]
    return accumulated / weight_sum


def body(
    hidden,
    lengths,
    prefix_id,
    placement_perm,
    prefix_owner,
    prefix_cache,
    qkv_weight,
    q_gain,
    k_gain,
    out_weight,
    attn_gain,
    gate_up_weight,
    down_weight,
    mlp_gain,
):
    tensor_rank = lax.axis_index("tensor")
    group_index = lax.axis_index("dp")
    slot_ids, live_slots, owner_req, offsets, prefix_pick = slot_plan(
        lengths, prefix_id, placement_perm, group_index
    )
    local_rows = hidden.shape[0]
    local_width = qkv_weight.shape[2]
    local_heads = local_width // HD
    row_start = tensor_rank * local_rows
    column_start = tensor_rank * local_width
    score_scale = HD ** (-0.5)
    full_rows = lax.all_gather(hidden, "tensor", axis=0, tiled=True)
    projected = jnp.einsum("cd,kde->kce", full_rows, qkv_weight, preferred_element_type=jnp.float32)
    norm_gains = jnp.stack(
        [
            lax.dynamic_slice_in_dim(q_gain, column_start, local_width),
            lax.dynamic_slice_in_dim(k_gain, column_start, local_width),
        ]
    )
    squares = jnp.sum(projected[:2] * projected[:2], axis=2)
    totals = lax.psum(squares, "tensor")
    normed = projected[:2] * lax.rsqrt(totals / D + EPSILON)[:, :, None] * norm_gains[:, None, :]
    queries = rotate(normed[0].reshape(CAP, local_heads, HD), offsets).astype(jnp.bfloat16)
    key_heads = rotate(normed[1].reshape(CAP, local_heads, HD), offsets).astype(jnp.bfloat16)
    value_heads = projected[2].astype(jnp.bfloat16).reshape(CAP, local_heads, HD)
    suf_scores = (
        jnp.einsum("chd,khd->hck", queries, key_heads, preferred_element_type=jnp.float32)
        * score_scale
    )
    visible = (
        (owner_req[:, None] == owner_req[None, :])
        & live_slots[None, :]
        & (slot_ids[None, :] <= slot_ids[:, None])
    )
    suf_scores = jnp.where(visible[None], suf_scores, MASKED_SCORE)
    partials = [partial_softmax(suf_scores, value_heads)]
    for prefix_num in range(2):
        prefix_kv = from_root(prefix_cache[0], "dp", prefix_owner[prefix_num])
        prefix_keys = prefix_kv[0].reshape(PLEN, local_heads, HD)
        prefix_values = prefix_kv[1].reshape(PLEN, local_heads, HD)
        pre_scores = (
            jnp.einsum("chd,khd->hck", queries, prefix_keys, preferred_element_type=jnp.float32)
            * score_scale
        )
        pre_scores = jnp.where((prefix_pick == prefix_num)[None, :, None], pre_scores, MASKED_SCORE)
        partials.append(partial_softmax(pre_scores, prefix_values))
    attended = merge_partials(partials).astype(jnp.bfloat16)
    attended = attended.transpose(1, 0, 2).reshape(CAP, local_width)
    summed = lax.psum(
        jnp.dot(attended, out_weight, preferred_element_type=jnp.float32).astype(jnp.bfloat16),
        "tensor",
    ).astype(jnp.float32)
    merged = (full_rows.astype(jnp.float32) + rms_scale(summed, attn_gain)).astype(jnp.bfloat16)
    mid_rows = lax.dynamic_slice_in_dim(merged, row_start, local_rows, 0)
    gate_up = jnp.einsum("cd,kdf->kcf", merged, gate_up_weight, preferred_element_type=jnp.float32)
    activated = (jax.nn.silu(gate_up[0]) * gate_up[1]).astype(jnp.bfloat16)
    mlp_term = lax.psum_scatter(
        jnp.dot(activated, down_weight, preferred_element_type=jnp.float32).astype(jnp.bfloat16),
        "tensor",
        scatter_dimension=0,
        tiled=True,
    ).astype(jnp.float32)
    result = mid_rows.astype(jnp.float32) + rms_scale(mlp_term, mlp_gain)
    live_rows = lax.dynamic_slice_in_dim(live_slots, row_start, local_rows, 0)
    hidden_out = jnp.where(live_rows[:, None], result, 0.0).astype(jnp.bfloat16)
    key_out = jnp.where(live_slots[:, None], key_heads.reshape(CAP, local_width), 0.0)
    value_out = jnp.where(live_slots[:, None], value_heads.reshape(CAP, local_width), 0.0)
    suffix_kv = jnp.stack([key_out, value_out])
    return (hidden_out, suffix_kv)


def solution(mesh):
    in_specs = (
        P(("dp", "tensor"), None),
        P(),
        P(),
        P(),
        P(),
        P("dp", None, None, "tensor"),
        P(None, None, "tensor"),
        P(),
        P(),
        P("tensor", None),
        P(),
        P(None, None, "tensor"),
        P("tensor", None),
        P(),
    )
    out_specs = (P(("dp", "tensor"), None), P(None, "dp", "tensor"))
    return jax.shard_map(body, mesh=mesh, in_specs=in_specs, out_specs=out_specs, check_vma=False)
```

profile of v0, /device:TPU:8, one launch (start us, length us, event | category | flops | bytes accessed | tf_op | source)
XLA Modules:
  0.0 571.1 jit_solution(1590346645159021836)
XLA Ops:
  8.0 0.0 copy-start
  8.0 0.0 all-gather.2.cloned.1.call-start
  8.1 0.7 all-gather.2.cloned.1.call-update
  8.7 0.0 all-reduce.6.cloned.1.call-start
  8.8 1.3 fusion.90
  11.4 4.0 select_bitcast_fusion.1
  15.4 0.0 all-reduce.6.cloned.1.call-update
  15.4 0.0 all-reduce.4.cloned.1.call-start
  15.5 0.6 copy-done.14
  16.1 0.1 compare_select_fusion
  16.1 0.0 copy-done.1
  16.1 0.6 gather_fusion
  16.8 0.1 fusion.81
  16.9 0.2 reduce-window.8
  17.0 0.0 copy-done.2
  17.0 0.6 gather_fusion.1
  17.7 0.8 dynamic-slice_bitcast_fusion
  18.5 0.1 broadcast_select_fusion.1
  18.6 0.1 convert_reduce_fusion
  18.7 65.7 %all-gather.2.cloned.1.call-done = bf16[768,2048]{1,0:T(8,128)(2,1)} async-done(((bf16[48,2048]{1,0:T(8,128)(2,1)}), bf16[768,2048]{1,0:T(8,128)(2,1)}) %all-gather.2.cloned.1.call-update) | async-done | bytes 3145744 | tf_op jit(solution)/shard_map/all_gather | solution.py:109
  84.5 3.8 fusion.26
  88.3 0.1 multiply_reduce_fusion
  88.3 43.7 %psum.28 = f32[2,768]{1,0:T(2,128)S(1)} all-reduce(f32[2,768]{1,0:T(2,128)S(1)} %multiply_reduce_fusion), channel_id=1, replica_groups=mesh['dp'=16,'tensor'=16] {'tensor'}, use_global_device_ids=true, to_apply=%region_4.6 | all-reduce | flops 1536 | bytes 12288 | tf_op jit(solution)/shard_map/psum | solution.py:118
  132.0 0.1 multiply_multiply_fusion
  132.2 0.1 slice_bitcast_fusion.10
  132.2 0.8 fusion.67
  133.1 0.0 copy-start.8
  133.1 0.0 copy-start.10
  133.1 0.6 copy-done.8
  133.7 0.7 fusion.91
  134.5 0.0 copy-done.10
  134.5 0.0 copy-start.4
  134.5 1.4 copy-done.4
  135.9 0.4 fusion.19
  136.3 78.6 %all-reduce.6.cloned.1.call-done = (bf16[2,4096,128]{2,1,0:T(8,128)(2,1)}, bf16[2,4096,128]{2,1,0:T(8,128)(2,1)}) async-done(((bf16[2,4096,128]{2,1,0:T(8,128)(2,1)}, bf16[2,4096,128]{2,1,0:T(8,128)(2,1)}), (bf16[2,4096,128]{2,1,0:T(8,128)(2,1)}, bf16[2,4096,128]{2,1,0:T(8,128)(2,1)})) %all-reduce.6.cloned.1.call-update) | async-done | bytes 4194320 | tf_op jit(solution)/shard_map/psum | solution.py:18
  214.9 4.5 fusion
  219.4 3.2 fusion.2
  222.5 0.0 copy-done.6
  222.5 3.2 fusion.1
  225.7 3.4 fusion.4
  229.1 0.0 copy-done.7
  229.1 3.5 fusion.32
  232.7 3.5 fusion.35
  236.1 5.6 convolution_convert_fusion.1
  241.8 0.0 all-reduce.4.cloned.1.call-update
  241.8 0.3 reduce-scatter.2.cloned.1.call-start
  242.1 208.5 %all-reduce.4.cloned.1.call-done = bf16[768,2048]{1,0:T(8,128)(2,1)} async-done(((bf16[768,2048]{1,0:T(8,128)(2,1)}), bf16[768,2048]{1,0:T(8,128)(2,1)}) %all-reduce.4.cloned.1.call-update) | async-done | bytes 3145744 | tf_op jit(solution)/shard_map/psum | solution.py:146
  450.6 2.7 fusion.6
  453.4 0.0 copy-done.12
  453.4 0.1 copy-done.3
  453.5 3.8 fusion.9
  457.3 0.0 copy-done.15
  457.3 0.0 copy-start.5
  457.3 3.4 fusion.21
  460.8 3.5 convolution_convert_fusion
  464.3 0.0 reduce-scatter.2.cloned.1.call-update
  464.3 0.1 dynamic_slice.16
  464.4 0.8 copy-done.9
  465.2 0.0 copy-done.11
  465.2 0.1 maximum_select_fusion
  465.3 0.9 copy.21
  466.3 94.8 %reduce-scatter.2.cloned.1.call-done = bf16[48,2048]{1,0:T(8,128)(2,1)} async-done(((bf16[768,2048]{1,0:T(8,128)(2,1)}), bf16[48,2048]{1,0:T(8,128)(2,1)}) %reduce-scatter.2.cloned.1.call-update) | async-done | bytes 196624 | tf_op jit(solution)/shard_map/reduce_scatter | solution.py:154
  561.0 1.1 fusion.49
  562.1 1.9 fusion.53
  (26 shorter events, 0.2 us)
Async XLA Ops:
  8.0 452.8 %copy-start = (bf16[512,2048]{1,0:T(8,128)(2,1)S(1)}, bf16[512,2048]{1,0:T(8,128)(2,1)}, u32[]{:S(2)}) copy-start(bf16[512,2048]{1,0:T(8,128)(2,1)} %param.28) | copy-start | bytes 6291460
  8.0 76.4 %all-gather.2.cloned.1.call-start = ((), (), s32[]{:S(2)}) async-start(), calls=%async_computation.1 | async-start | bytes 3342336 | tf_op jit(solution)/shard_map/all_gather | solution.py:109
  8.7 206.2 %all-reduce.6.cloned.1.call-start = ((), (), s32[]{:S(2)}) async-start(), calls=%async_computation.4 | async-start | bytes 8388608 | tf_op jit(solution)/shard_map/psum | solution.py:18
  15.4 0.7 copy-start.14
  15.4 0.7 copy-start.1
  15.4 1.6 copy-start.2
  15.4 435.2 %all-reduce.4.cloned.1.call-start = ((), (), s32[]{:S(2)}) async-start(), calls=%async_computation.2 | async-start | bytes 6291456 | tf_op jit(solution)/shard_map/psum | solution.py:146
  133.1 0.6 copy-start.8
  133.1 1.4 copy-start.10
  134.5 1.5 copy-start.4
  219.4 3.2 copy-start.6
  225.7 3.4 copy-start.7
  241.8 211.6 %copy-start.12 = (f32[2048]{0:T(1024)S(1)}, f32[2048]{0:T(1024)}, u32[]{:S(2)}) copy-start(f32[2048]{0:T(1024)} %param.26) | copy-start | bytes 24580
  241.8 319.3 %reduce-scatter.2.cloned.1.call-start = ((), (), s32[]{:S(2)}) async-start(), calls=%async_computation.3 | async-start | bytes 3342336 | tf_op jit(solution)/shard_map/reduce_scatter | solution.py:154
  450.6 2.8 copy-start.3
  453.5 3.9 copy-start.15
  457.3 3.4 copy-start.5
  464.3 0.9 copy-start.9
  464.3 0.9 copy-start.11
  464.3 97.8 %copy-start.13 = (f32[2048]{0:T(1024)S(1)}, f32[2048]{0:T(1024)}, u32[]{:S(2)}) copy-start(f32[2048]{0:T(1024)} %param.29) | copy-start | bytes 24580
Sparse Core Ops, SparseCore 0:
  11.5 72.8 all-gather.1
  241.9 208.6 all-reduce.3
  464.4 96.5 reduce-scatter.1
Sparse Core Ops, SparseCore 1:
  15.5 199.3 all-reduce.5
where the time goes:
time: 571 us
  waiting for transfers between devices  448 us (78%)
  blocking collectives  43.7 us (8%)
  matrix products  31.7 us (6%)
  other arithmetic  22.2 us (4%)
  between operations  16.8 us (3%)
  local copies, waits for them, and re-layouts  8.02 us (1%)
    psum x1, waiting for transfers between devices, body(): lax.psum(jnp.dot(attended, out_weight, preferred_element_type=jnp.float32...  209 us
    reduce_scatter x1, waiting for transfers between devices, body(): lax.psum_scatter(jnp.dot(activated, down_weight, preferred_element_type=j...  94.8 us
    psum x1, waiting for transfers between devices, from_root(): return lax.psum(jnp.where(mine, shard, jnp.zeros_like(shard)), axis)  78.6 us
    all_gather x1, waiting for transfers between devices, body(): full_rows = lax.all_gather(hidden, 'tensor', axis=0, tiled=True)  65.7 us
    psum x1, blocking collectives, body(): totals = lax.psum(squares, 'tensor')  43.7 us
  transfers between devices with their start and end apart: 4, of which 4 were waited for; matrix products, arithmetic and copies ran while one was open for 3% of the time, Pallas kernels for 0%

commit v1 on v0

--- a/solution.py
+++ b/solution.py
@@ -106,7 +106,9 @@
     row_start = tensor_rank * local_rows
     column_start = tensor_rank * local_width
     score_scale = HD ** (-0.5)
-    full_rows = lax.all_gather(hidden, "tensor", axis=0, tiled=True)
+    full_rows = jnp.concatenate(
+        lax.all_to_all(jnp.stack([hidden] * lax.axis_size("tensor")), "tensor", 0, 0), axis=0
+    )
     projected = jnp.einsum("cd,kde->kce", full_rows, qkv_weight, preferred_element_type=jnp.float32)
     norm_gains = jnp.stack(
         [

time: 571 us -> 600 us (1.051)
  waiting for transfers between devices: 448 us -> 464 us
  starting transfers between devices: 0.42 us -> 11.6 us
    all_to_all x0 -> x1, waiting for transfers between devices: none -> 66.8 us  [body(): lax.all_to_all(jnp.stack([hidden] * lax.axis_size('tensor')), 'tensor', 0...]
    all_gather x1 -> x0, waiting for transfers between devices: 65.7 us -> none  [body(): full_rows = lax.all_gather(hidden, 'tensor', axis=0, tiled=True)]
    all_to_all x0 -> x1, starting transfers between devices: none -> 11.2 us  [body(): lax.all_to_all(jnp.stack([hidden] * lax.axis_size('tensor')), 'tensor', 0...]
    psum x1, waiting for transfers between devices: 78.6 us -> 89.8 us  [from_root(): return lax.psum(jnp.where(mine, shard, jnp.zeros_like(shard)), axis)]
  transfers between devices with their start and end apart: 4 -> 4, of which waited for: 4 -> 4; matrix products, arithmetic and copies ran while one was open for 3% -> 2% of each run, Pallas kernels for 0% -> 0%
where the time goes in v1:
time: 600 us
  waiting for transfers between devices  464 us (77%)
  blocking collectives  43.6 us (7%)
  matrix products  33 us (6%)
  other arithmetic  22.8 us (4%)
  between operations  15.3 us (3%)
  starting transfers between devices  11.6 us (2%)
  local copies, waits for them, and re-layouts  9.8 us (2%)
    psum x1, waiting for transfers between devices, body(): lax.psum(jnp.dot(attended, out_weight, preferred_element_type=jnp.float32...  212 us
    reduce_scatter x1, waiting for transfers between devices, body(): lax.psum_scatter(jnp.dot(activated, down_weight, preferred_element_type=j...  94.8 us
    psum x1, waiting for transfers between devices, from_root(): return lax.psum(jnp.where(mine, shard, jnp.zeros_like(shard)), axis)  89.8 us
    all_to_all x1, waiting for transfers between devices, body(): lax.all_to_all(jnp.stack([hidden] * lax.axis_size('tensor')), 'tensor', 0...  66.8 us
    psum x1, blocking collectives, body(): totals = lax.psum(squares, 'tensor')  43.6 us
  transfers between devices with their start and end apart: 4, of which 4 were waited for; matrix products, arithmetic and copies ran while one was open for 2% of the time, Pallas kernels for 0%

profile of v1, /device:TPU:8, one launch (start us, length us, event | category | flops | bytes accessed | tf_op | source)
XLA Modules:
  0.0 600.0 jit_solution(10426058517906021504)
XLA Ops:
  7.2 0.0 copy-start
  7.2 3.1 stack.10
  10.3 11.2 %all-to-all-start = ((bf16[16,48,2048]{2,1,0:T(8,128)(2,1)}), bf16[16,48,2048]{2,1,0:T(8,128)(2,1)}, u32[]{:S(2)}, u32[]{:S(2)}) async-start(bf16[16,48,2048]{2,1,0:T(8,128)(2,1)} %stack.10), calls=%async_computation | async-start | bytes 6291456 | tf_op jit(solution)/shard_map/all_to_all | solution.py:110
  21.5 0.0 all-reduce.6.cloned.1.call-start
  21.6 0.0 copy-done.13
  21.6 0.6 fusion.85
  23.5 3.9 select_bitcast_fusion.1
  27.4 0.0 all-reduce.6.cloned.1.call-update
  27.4 0.0 all-reduce.4.cloned.1.call-start
  27.5 0.6 copy-done.14
  28.1 0.1 compare_select_fusion
  28.1 0.0 copy-done.1
  28.1 0.6 gather_fusion
  28.8 0.1 fusion.76
  28.9 0.2 reduce-window.8
  29.0 0.0 copy-done.2
  29.1 0.6 gather_fusion.1
  29.7 0.8 dynamic-slice_bitcast_fusion
  30.5 0.1 broadcast_select_fusion.1
  30.6 0.1 convert_reduce_fusion
  30.7 66.8 %all-to-all-done = bf16[16,48,2048]{2,1,0:T(8,128)(2,1)} async-done(((bf16[16,48,2048]{2,1,0:T(8,128)(2,1)}), bf16[16,48,2048]{2,1,0:T(8,128)(2,1)}, u32[]{:S(2)}, u32[]{:S(2)}) %all-to-all-start) | async-done | bytes 3145760 | tf_op jit(solution)/shard_map/all_to_all | solution.py:110
  97.6 3.8 convolution_bitcast_fusion
  101.4 0.1 multiply_reduce_fusion
  101.5 43.6 %psum.28 = f32[2,768]{1,0:T(2,128)S(1)} all-reduce(f32[2,768]{1,0:T(2,128)S(1)} %multiply_reduce_fusion), channel_id=1, replica_groups=mesh['dp'=16,'tensor'=16] {'tensor'}, use_global_device_ids=true, to_apply=%region_4.6 | all-reduce | flops 1536 | bytes 12288 | tf_op jit(solution)/shard_map/psum | solution.py:120
  145.2 0.1 multiply_multiply_fusion
  145.3 0.1 slice_bitcast_fusion.10
  145.4 1.5 fusion.62
  146.9 89.8 %all-reduce.6.cloned.1.call-done = (bf16[2,4096,128]{2,1,0:T(8,128)(2,1)}, bf16[2,4096,128]{2,1,0:T(8,128)(2,1)}) async-done(((bf16[2,4096,128]{2,1,0:T(8,128)(2,1)}, bf16[2,4096,128]{2,1,0:T(8,128)(2,1)}), (bf16[2,4096,128]{2,1,0:T(8,128)(2,1)}, bf16[2,4096,128]{2,1,0:T(8,128)(2,1)})) %all-reduce.6.cloned.1.call-update) | async-done | bytes 4194320 | tf_op jit(solution)/shard_map/psum | solution.py:18
  236.7 4.5 fusion.1
  241.1 3.2 fusion.4
  244.3 0.0 copy-done.6
  244.3 3.1 fusion
  247.5 0.0 copy-start.7
  247.5 0.0 copy-start.9
  247.5 3.4 fusion.2
  250.9 0.0 copy-done.7
  250.9 0.0 copy-done.9
  250.9 0.7 fusion.86
  251.6 0.0 copy-start.4
  251.7 1.4 copy-done.4
  253.1 0.4 fusion.17
  253.5 4.8 fusion.30
  258.2 3.5 fusion.27
  261.8 5.6 convolution_convert_fusion.1
  267.4 0.0 all-reduce.4.cloned.1.call-update
  267.4 0.3 reduce-scatter.2.cloned.1.call-start
  267.7 212.5 %all-reduce.4.cloned.1.call-done = bf16[768,2048]{1,0:T(8,128)(2,1)} async-done(((bf16[768,2048]{1,0:T(8,128)(2,1)}), bf16[768,2048]{1,0:T(8,128)(2,1)}) %all-reduce.4.cloned.1.call-update) | async-done | bytes 3145744 | tf_op jit(solution)/shard_map/psum | solution.py:148
  480.2 2.7 fusion.6
  482.9 0.0 copy-done.11
  482.9 0.1 copy-done.3
  483.0 3.8 fusion.9
  486.8 0.0 copy-done.15
  486.8 0.0 copy-start.5
  486.9 3.4 fusion.19
  490.3 3.5 convolution_convert_fusion
  493.8 0.0 reduce-scatter.2.cloned.1.call-update
  493.8 0.1 dynamic_slice.16
  493.9 0.8 copy-done.8
  494.7 0.0 copy-done.10
  494.7 0.1 maximum_select_fusion
  494.9 0.9 copy.21
  495.8 94.8 %reduce-scatter.2.cloned.1.call-done = bf16[48,2048]{1,0:T(8,128)(2,1)} async-done(((bf16[768,2048]{1,0:T(8,128)(2,1)}), bf16[48,2048]{1,0:T(8,128)(2,1)}) %reduce-scatter.2.cloned.1.call-update) | async-done | bytes 196624 | tf_op jit(solution)/shard_map/reduce_scatter | solution.py:156
  590.6 1.1 fusion.44
  591.6 1.9 fusion.48
  (26 shorter events, 0.2 us)
Async XLA Ops:
  7.2 483.1 %copy-start = (bf16[512,2048]{1,0:T(8,128)(2,1)S(1)}, bf16[512,2048]{1,0:T(8,128)(2,1)}, u32[]{:S(2)}) copy-start(bf16[512,2048]{1,0:T(8,128)(2,1)} %param.28) | copy-start | bytes 6291460
  10.3 11.3 %copy-start.13 = (s32[2]{0:T(128)S(1)}, s32[2]{0:T(128)}, u32[]{:S(2)}) copy-start(s32[2]{0:T(128)} %param.20) | copy-start | bytes 28
  10.3 87.3 %all-to-all-start = ((bf16[16,48,2048]{2,1,0:T(8,128)(2,1)}), bf16[16,48,2048]{2,1,0:T(8,128)(2,1)}, u32[]{:S(2)}, u32[]{:S(2)}) async-start(bf16[16,48,2048]{2,1,0:T(8,128)(2,1)} %stack.10), calls=%async_computation | async-start | bytes 6291456 | tf_op jit(solution)/shard_map/all_to_all | solution.py:110
  21.5 215.1 %all-reduce.6.cloned.1.call-start = ((), (), s32[]{:S(2)}) async-start(), calls=%async_computation.4 | async-start | bytes 8388608 | tf_op jit(solution)/shard_map/psum | solution.py:18
  27.4 0.7 copy-start.14
  27.4 0.7 copy-start.1
  27.4 1.6 copy-start.2
  27.4 452.7 %all-reduce.4.cloned.1.call-start = ((), (), s32[]{:S(2)}) async-start(), calls=%async_computation.2 | async-start | bytes 6291456 | tf_op jit(solution)/shard_map/psum | solution.py:148
  241.1 3.2 copy-start.6
  247.5 3.4 copy-start.7
  247.5 3.4 copy-start.9
  251.6 1.4 copy-start.4
  267.4 215.5 %copy-start.11 = (f32[2048]{0:T(1024)S(1)}, f32[2048]{0:T(1024)}, u32[]{:S(2)}) copy-start(f32[2048]{0:T(1024)} %param.26) | copy-start | bytes 24580
  267.4 323.2 %reduce-scatter.2.cloned.1.call-start = ((), (), s32[]{:S(2)}) async-start(), calls=%async_computation.3 | async-start | bytes 3342336 | tf_op jit(solution)/shard_map/reduce_scatter | solution.py:156
  480.2 2.8 copy-start.3
  483.0 3.9 copy-start.15
  486.8 3.4 copy-start.5
  493.8 0.9 copy-start.8
  493.8 0.9 copy-start.10
  493.8 97.8 %copy-start.12 = (f32[2048]{0:T(1024)S(1)}, f32[2048]{0:T(1024)}, u32[]{:S(2)}) copy-start(f32[2048]{0:T(1024)} %param.29) | copy-start | bytes 24580
Sparse Core Ops, SparseCore 0:
  27.6 209.0 all-reduce.5
  267.5 212.6 all-reduce.3
  494.0 96.5 reduce-scatter.1
